TPU v7x, 256 devices: a whole 4x4x8 slice. The times are simulated.
256 devices in a mesh: req: 32 (over x, y, core), kv: 8 (over z).
Axes of the slice: x: 4, y: 4, z: 8, core: 2. Of those that a mesh axis runs over, the one named last changes fastest.
Arguments:
- hidden: bfloat16 [512, 1536], P('req'), may hold values from -6 to 6
- norm_gain: float32 [1536], replicated, may hold values from 0.5 to 1.5
- w_qkv: bfloat16 [1536, 3072], P(None, 'kv'), may hold values from -0.15625 to 0.15625
- w_out: bfloat16 [1536, 1536], P(None, 'kv'), may hold values from -0.15625 to 0.15625
- cache_pages: bfloat16 [6144, 2, 8, 96, 128], P('req', None, 'kv'), may hold values from -340 to 340
- lengths: int32 [512], P('req'), may hold values from 1 to 16384, as said below
- page_table: int32 [512, 128], P('req'), may hold values from 0 to 191, as said below
- occupant: int32 [512], replicated, may hold values from 0 to 511, each once
Outputs:
- mixed: bfloat16 [512, 1536], P('req', 'kv')
Inputs may be any that keep to these rules, and one draw needn't show every extreme that they name: `occupant`: every request is served at exactly one slot. Slot s holds ceil(lengths[s] / 128) pages; on every index of req the pages of its 16 slots fit its pool of 192, some pool is full, and some request has 16384 tokens. `page_table`: the first ceil(lengths[s] / 128) entries of slot s are pages of its own pool that no other slot of that pool uses; later entries are arbitrary pages of the pool.
All inputs are finite; a program needn't handle non-finite values.
Results may differ from a plain program's by a relative error of at most 0.0043.
Values may be sent and summed in bfloat16 or wider, within the bound.
No kernel may reach another device: no remote copies, remote signals or barrier semaphores. Data moves between devices by JAX's collectives and lax.ppermute only.
A program may use at most 64 MiB of HBM per device.

v0:
```python
import math
import jax
import jax.numpy as jnp
from jax import lax
from jax.sharding import PartitionSpec as P

HD = 96
PAGE = 128
MAXP = 128
GROUP = 2


def per_device(hidden, norm_gain, w_qkv, w_out, cache_pages, lengths, page_table, occupant):
    slot_count = hidden.shape[0]
    pool_size = cache_pages.shape[0]
    kv_local = cache_pages.shape[2]
    first_slot = lax.axis_index("req") * slot_count
    hidden_wide = hidden.astype(jnp.float32)
    normed = (
        hidden_wide
        * lax.rsqrt(jnp.mean(hidden_wide * hidden_wide, axis=1, keepdims=True) + 1e-05)
        * norm_gain
    ).astype(jnp.bfloat16)
    served = lax.dynamic_slice_in_dim(occupant, first_slot, slot_count)
    every_normed = lax.all_gather(normed, "req", axis=0, tiled=True)
    picked = jnp.take(every_normed, served, axis=0)
    slot_rows = jnp.dot(picked, w_qkv, preferred_element_type=jnp.float32).astype(jnp.bfloat16)
    slot_rows = slot_rows.reshape(slot_count, kv_local, GROUP + 2, HD)
    queries = slot_rows[:, :, :GROUP]
    own_key = slot_rows[:, :, GROUP]
    own_value = slot_rows[:, :, GROUP + 1]
    score_scale = 1.0 / math.sqrt(HD)
    pages_used = (lengths + PAGE - 1) // PAGE
    live_page = jnp.arange(MAXP, dtype=jnp.int32)[None, :] < pages_used[:, None]
    matches = (
        (page_table[:, :, None] == jnp.arange(pool_size, dtype=jnp.int32)[None, None, :])
        & live_page[:, :, None]
    ).astype(jnp.int32)
    owner_table = jnp.sum(matches, axis=1)
    slot_ids = jnp.arange(slot_count, dtype=jnp.int32)
    page_owner = jnp.sum(owner_table * slot_ids[:, None], axis=0)
    page_rank = jnp.sum(matches * jnp.arange(MAXP, dtype=jnp.int32)[None, :, None], axis=(0, 1))
    page_limit = jnp.sum(owner_table * lengths[:, None], axis=0)
    offsets = page_rank[:, None] * PAGE + jnp.arange(PAGE, dtype=jnp.int32)[None, :]
    token_live = offsets < page_limit[:, None]
    page_queries = jnp.take(queries, page_owner, axis=0)
    scores = (
        jnp.einsum(
            "pgjd,pgdt->pgjt", page_queries, cache_pages[:, 0], preferred_element_type=jnp.float32
        )
        * score_scale
    )
    scores = jnp.where(token_live[:, None, None, :], scores, -jnp.inf)
    page_max = jnp.max(scores, axis=-1)
    own_score = (
        jnp.sum(queries.astype(jnp.float32) * own_key.astype(jnp.float32)[:, :, None, :], axis=-1)
        * score_scale
    )
    owner_mask = owner_table > 0
    slot_max = jnp.max(jnp.where(owner_mask[:, :, None, None], page_max[None], -jnp.inf), axis=1)
    slot_max = jnp.maximum(slot_max, own_score)
    weights = jnp.exp(scores - jnp.take(slot_max, page_owner, axis=0)[..., None])
    rounded = weights.astype(jnp.bfloat16)
    page_total = jnp.sum(weights, axis=-1)
    page_numerator = jnp.einsum(
        "pgjt,pgdt->pgjd", rounded, cache_pages[:, 1], preferred_element_type=jnp.float32
    )
    own_weight = jnp.exp(own_score - slot_max)
    own_rounded = lax.optimization_barrier(own_weight.astype(jnp.bfloat16)).astype(jnp.float32)
    owner_float = owner_table.astype(jnp.float32)
    denominator = (
        jnp.einsum("sp,pgj->sgj", owner_float, page_total, precision=lax.Precision.HIGHEST)
        + own_weight
    )
    numerator = jnp.einsum(
        "sp,pgjd->sgjd", owner_float, page_numerator, precision=lax.Precision.HIGHEST
    )
    numerator = numerator + own_rounded[..., None] * own_value.astype(jnp.float32)[:, :, None, :]
    context = (numerator / denominator[..., None]).astype(jnp.bfloat16).reshape(slot_count, -1)
    gathered = lax.all_gather(context, "req", axis=0, tiled=True)
    wanted = first_slot + slot_ids
    selector = (occupant[None, :] == wanted[:, None]).astype(jnp.bfloat16)
    attended = jnp.dot(selector, gathered, preferred_element_type=jnp.float32).astype(jnp.bfloat16)
    partial_value = lax.dot_general(
        attended, w_out, (((1,), (1,)), ((), ())), preferred_element_type=jnp.float32
    )
    summed = lax.psum_scatter(partial_value, "kv", scatter_dimension=1, tiled=True)
    col_share = summed.shape[1]
    residual = lax.dynamic_slice_in_dim(hidden_wide, lax.axis_index("kv") * col_share, col_share, 1)
    return (residual + summed).astype(jnp.bfloat16)


def solution(mesh):
    return jax.shard_map(
        per_device,
        mesh=mesh,
        in_specs=(
            P("req", None),
            P(),
            P(None, "kv"),
            P(None, "kv"),
            P("req", None, "kv", None, None),
            P("req"),
            P("req", None),
            P(),
        ),
        out_specs=P("req", "kv"),
        check_vma=False,
    )
```

profile of v0, /device:TPU:2, one launch (start us, length us, event | category | flops | bytes accessed | tf_op | source)
XLA Modules:
  0.0 147.1 jit_solution(2917014156746804395)
XLA Ops:
  6.5 0.0 copy-start
  6.5 0.0 all-gather.2.cloned.1.call-start
  6.5 1.0 multiply_reduce_fusion
  7.6 1.5 %multiply_convert_fusion = bf16[16,1536]{1,0:T(8,128)(2,1)} fusion(f32[1536]{0:T(1024)} %param.9, f32[16]{0:T(128)S(1)} %add_rsqrt_fusion, bf16[16,1536]{1,0:T(8,128)(2,1)} %param.8), kind=kLoop, calls=%fused_computation.28 | loop fusion | flops 98304 | bytes 104512 | tf_op jit(solution)/shard_map/convert_element_type | solution.py:23
  9.1 0.0 all-gather.2.cloned.1.call-update
  9.1 0.0 reduce-scatter.4.cloned.1.call-start
  9.2 0.8 compare_and_fusion
  10.0 0.7 and_select_fusion
  10.6 0.1 iota_compare_fusion.1
  10.7 1.7 %select_reduce_fusion = (s32[192]{0:T(256)S(1)}, s32[16,192]{1,0:T(8,128)S(1)}) fusion(s32[16,128]{1,0:T(8,128)} %param.14, pred[16,128]{1,0:T(8,128)(4,1)S(1)} %iota_compare_fusion.1), kind=kLoop, calls=%fused_computation.10 | loop fusion | flops 2356032 | bytes 23296 | tf_op jit(solution)/shard_map/reduce_sum | solution.py:42
  12.4 0.7 multiply_reduce_fusion.2
  13.2 0.1 add_compare_fusion
  13.3 47.2 %all-gather.2.cloned.1.call-done = bf16[512,1536]{1,0:T(8,128)(2,1)} async-done(((bf16[16,1536]{1,0:T(8,128)(2,1)}), bf16[512,1536]{1,0:T(8,128)(2,1)}) %all-gather.2.cloned.1.call-update) | async-done | bytes 1572880 | tf_op jit(solution)/shard_map/all_gather | solution.py:25
  60.5 2.2 %gather_fusion = bf16[16,1536]{1,0:T(8,128)(2,1)S(1)} fusion(bf16[512,1536]{1,0:T(8,128)(2,1)} %all-gather.2.cloned.1.call-done, s32[1024]{0:T(1024)S(1)} %pad_clamp_fusion.1), kind=kCustom, calls=%fused_computation | custom fusion | bytes 98368 | tf_op jit(solution)/shard_map/jit(_take)/gather | solution.py:26
  62.7 0.0 copy-done
  62.7 0.3 convolution_convert_fusion
  63.1 0.1 reshape.230
  63.2 0.1 multiply_reduce_fusion.1
  63.3 0.1 copy.28
  63.4 0.8 gather_fusion.1
  64.2 3.8 %fusion.39 = (f32[192,2]{1,0:T(8,128)S(1)}, f32[192,2,128]{2,1,0:T(2,128)S(1)}) fusion(bf16[192,2,1,96,128]{4,3,2,1,0:T(8,128)(2,1)} %param.12, bf16[192,2,96]{2,1,0:T(2,128)(2,1)S(1)} %gather_fusion.1, pred[192]{0:T(512)(128)(4,1)S(1)} %compare_and_fusion.1, pred[192,128]{1,0:T(8,128)(4,1)S(1)} %add_compare_fusion), kind=kOutput, calls=%fused_computation.76 | convolution fusion | flops 9621120 | bytes 5015232 | tf_op jit(solution)/shard_map/pgjd,pgdt->pgjt/dot_general | solution.py:48
  68.1 0.1 copy.27
  68.2 0.1 select_reduce_fusion.1
  68.3 0.1 copy.29
  68.4 0.7 gather_fusion.2
  69.1 0.1 broadcast_select_fusion.2
  69.2 0.0 copy-start.1
  69.2 0.0 copy-start.3
  69.2 5.0 %fusion = f32[192,2,96]{2,1,0:T(2,128)S(1)} fusion(bf16[192,2,1,96,128]{4,3,2,1,0:T(8,128)(2,1)} %param.12, f32[192,2,128]{2,1,0:T(2,128)S(1)} %get-tuple-element.16, f32[192,2]{1,0:T(8,128)S(1)} %broadcast_select_fusion.2), kind=kOutput, calls=%fused_computation.3 | convolution fusion | flops 9535488 | bytes 5064192 | tf_op jit(solution)/shard_map/pgjt,pgdt->pgjd/dot_general | solution.py:65
  74.2 0.5 fusion.16
  74.7 0.0 copy-start.2
  74.8 0.3 convolution_add_fusion.1
  75.0 0.3 fusion.11
  75.3 0.1 reshape.233
  75.4 23.2 %all_gather.7 = bf16[512,192]{1,0:T(8,128)(2,1)S(1)} all-gather(bf16[16,192]{1,0:T(8,128)(2,1)S(1)} %reshape.233), channel_id=1, replica_groups=mesh['req'=32,'kv'=8] {'req'}, dimensions={0}, use_global_device_ids=true | all-gather | bytes 202752 | tf_op jit(solution)/shard_map/all_gather | solution.py:80
  98.6 0.0 copy-done.1
  98.6 0.0 copy-done.3
  98.6 1.5 %convolution_bitcast_fusion = f32[1536,16]{1,0:T(8,128)} fusion(bf16[1536,192]{0,1:T(8,128)(2,1)S(1)} %copy-done.1, bf16[512,192]{1,0:T(8,128)(2,1)S(1)} %all_gather.7, s32[512]{0:T(512)S(1)} %copy-done.3, s32[16]{0:T(128)S(1)} %iota_add_fusion), kind=kOutput, calls=%fused_computation.9 | convolution fusion | flops 12594176 | bytes 886848
  100.1 0.0 reduce-scatter.4.cloned.1.call-update
  100.1 0.0 copy-done.2
  100.2 38.5 %reduce-scatter.4.cloned.1.call-done = f32[192,16]{1,0:T(8,128)} async-done(((f32[1536,16]{1,0:T(8,128)}), f32[192,16]{1,0:T(8,128)}) %reduce-scatter.4.cloned.1.call-update) | async-done | bytes 12304
  138.6 0.9 copy.34
  139.6 0.7 add_convert_fusion
  (14 shorter events, 0.1 us)
Async XLA Ops:
  6.5 56.2 %copy-start = (bf16[1536,384]{1,0:T(8,128)(2,1)S(1)}, bf16[1536,384]{1,0:T(8,128)(2,1)}, u32[]{:S(2)}) copy-start(bf16[1536,384]{1,0:T(8,128)(2,1)} %param.10) | copy-start | bytes 3538948
  6.5 53.9 %all-gather.2.cloned.1.call-start = ((), (), s32[]{:S(2)}) async-start(), calls=%async_computation.1 | async-start | bytes 1622016 | tf_op jit(solution)/shard_map/all_gather | solution.py:25
  9.1 129.5 %reduce-scatter.4.cloned.1.call-start = ((), (), s32[]{:S(2)}) async-start(), calls=%async_computation.2 | async-start | bytes 884736
  69.2 29.5 %copy-start.1 = (bf16[1536,192]{0,1:T(8,128)(2,1)S(1)}, bf16[1536,192]{0,1:T(8,128)(2,1)}, u32[]{:S(2)}) copy-start(bf16[1536,192]{0,1:T(8,128)(2,1)} %param.11) | copy-start | bytes 1769476
  69.2 29.4 %copy-start.3 = (s32[512]{0:T(512)S(1)}, s32[512]{0:T(512)}, u32[]{:S(2)}) copy-start(s32[512]{0:T(512)} %param.15) | copy-start | bytes 6148
  74.7 25.4 %copy-start.2 = (bf16[16,1536]{1,0:T(8,128)(2,1)S(1)}, bf16[16,1536]{1,0:T(8,128)(2,1)}, u32[]{:S(2)}) copy-start(bf16[16,1536]{1,0:T(8,128)(2,1)} %param.8) | copy-start | bytes 147460
Sparse Core Ops, SparseCore 0:
  9.9 50.5 all-gather.1
  100.2 38.3 reduce-scatter.3
where the time goes:
time: 147 us
  waiting for transfers between devices  85.7 us (58%)
  blocking collectives  23.2 us (16%)
  between operations  13.6 us (9%)
  matrix products  11.2 us (8%)
  other arithmetic  8.17 us (6%)
  local copies, waits for them, and re-layouts  5.21 us (4%)
    all_gather x1, waiting for transfers between devices, per_device(): every_normed = lax.all_gather(normed, 'req', axis=0, tiled=True)  47.2 us
    unnamed x3, waiting for transfers between devices  38.5 us
    all_gather x1, blocking collectives, per_device(): gathered = lax.all_gather(context, 'req', axis=0, tiled=True)  23.2 us
    dot_general x1, matrix products, per_device(): jnp.einsum('pgjt,pgdt->pgjd', rounded, cache_pages[:, 1], preferred_eleme...  5.01 us
    dot_general x1, matrix products, per_device(): jnp.einsum('pgjd,pgdt->pgjt', page_queries, cache_pages[:, 0], preferred_...  3.85 us
  transfers between devices with their start and end apart: 2, of which 2 were waited for; matrix products, arithmetic and copies ran while one was open for 3% of the time, Pallas kernels for 0%

commit v1 on v0

--- a/solution.py
+++ b/solution.py
@@ -22,7 +22,11 @@
         * norm_gain
     ).astype(jnp.bfloat16)
     served = lax.dynamic_slice_in_dim(occupant, first_slot, slot_count)
-    every_normed = lax.all_gather(normed, "req", axis=0, tiled=True)
+    length = lax.axis_size("req")
+    repeats = [length if d == 0 else 1 for d in range(normed.ndim)]
+    every_normed = lax.all_to_all(
+        jnp.tile(normed, repeats), "req", split_axis=0, concat_axis=0, tiled=True
+    )
     picked = jnp.take(every_normed, served, axis=0)
     slot_rows = jnp.dot(picked, w_qkv, preferred_element_type=jnp.float32).astype(jnp.bfloat16)
     slot_rows = slot_rows.reshape(slot_count, kv_local, GROUP + 2, HD)

time: 147 us -> 125 us (0.85)
  waiting for transfers between devices: 85.7 us -> 57.9 us
  starting transfers between devices: 0.04 us -> 7.8 us
  other arithmetic: 8.17 us -> 4.88 us
  blocking collectives: 23.2 us -> 24.9 us
    all_gather x1 -> x0, waiting for transfers between devices: 47.2 us -> none  [per_device(): every_normed = lax.all_gather(normed, 'req', axis=0, tiled=True)]
    all_to_all x0 -> x1, waiting for transfers between devices: none -> 18.6 us  [per_device(): lax.all_to_all(jnp.tile(normed, repeats), 'req', split_axis=0, concat_axi...]
    all_to_all x0 -> x1, starting transfers between devices: none -> 7.75 us  [per_device(): lax.all_to_all(jnp.tile(normed, repeats), 'req', split_axis=0, concat_axi...]
    gather x1, local copies, waits for them, and re-layouts: 2.25 us -> 0.59 us  [per_device(): picked = jnp.take(every_normed, served, axis=0)]
    all_gather x1, blocking collectives: 23.2 us -> 24.9 us  [per_device(): gathered = lax.all_gather(context, 'req', axis=0, tiled=True)]
    unnamed x3 -> x2, waiting for transfers between devices: 38.5 us -> 39.3 us
  transfers between devices with their start and end apart: 2 -> 2, of which waited for: 2 -> 2; matrix products, arithmetic and copies ran while one was open for 3% -> 1% of each run, Pallas kernels for 0% -> 0%
where the time goes in v1:
time: 125 us
  waiting for transfers between devices  57.9 us (46%)
  blocking collectives  24.9 us (20%)
  between operations  13.6 us (11%)
  matrix products  11.2 us (9%)
  starting transfers between devices  7.8 us (6%)
  local copies, waits for them, and re-layouts  4.89 us (4%)
  other arithmetic  4.88 us (4%)
    unnamed x2, waiting for transfers between devices  39.3 us
    all_gather x1, blocking collectives, per_device(): gathered = lax.all_gather(context, 'req', axis=0, tiled=True)  24.9 us
    all_to_all x1, waiting for transfers between devices, per_device(): lax.all_to_all(jnp.tile(normed, repeats), 'req', split_axis=0, concat_axi...  18.6 us
    all_to_all x1, starting transfers between devices, per_device(): lax.all_to_all(jnp.tile(normed, repeats), 'req', split_axis=0, concat_axi...  7.75 us
    dot_general x1, matrix products, per_device(): jnp.einsum('pgjt,pgdt->pgjd', rounded, cache_pages[:, 1], preferred_eleme...  5.01 us
    dot_general x1, matrix products, per_device(): jnp.einsum('pgjd,pgdt->pgjt', page_queries, cache_pages[:, 0], preferred_...  3.84 us
  transfers between devices with their start and end apart: 2, of which 2 were waited for; matrix products, arithmetic and copies ran while one was open for 1% of the time, Pallas kernels for 0%

profile of v1, /device:TPU:2, one launch (start us, length us, event | category | flops | bytes accessed | tf_op | source)
XLA Modules:
  0.0 125.1 jit_solution(12680022186596960200)
XLA Ops:
  6.5 0.0 copy-start
  6.5 1.0 multiply_reduce_fusion
  7.6 0.9 multiply_convert_fusion
  8.5 1.3 %tile.2 = bf16[32,16,1536]{2,1,0:T(8,128)(2,1)} broadcast(bf16[16,1536]{1,0:T(8,128)(2,1)S(1)} %multiply_convert_fusion), dimensions={1,2} | broadcast | bytes 1622016 | tf_op jit(solution)/shard_map/tile | solution.py:28
  9.8 0.0 copy-start.4
  9.8 0.0 copy-start.5
  9.8 0.0 copy-start.3
  9.8 7.8 %all-to-all-start = ((bf16[32,16,1536]{2,1,0:T(8,128)(2,1)}), bf16[32,16,1536]{2,1,0:T(8,128)(2,1)S(1)}, u32[]{:S(2)}, u32[]{:S(2)}) async-start(bf16[32,16,1536]{2,1,0:T(8,128)(2,1)} %tile.2), calls=%async_computation | async-start | bytes 3145728 | tf_op jit(solution)/shard_map/all_to_all | solution.py:27
  17.6 0.0 reduce-scatter.4.cloned.1.call-start
  17.6 0.0 copy-done.4
  17.6 0.1 compare_and_fusion
  17.7 0.0 copy-done.5
  17.8 0.1 iota_compare_fusion.1
  17.8 0.0 copy-done.3
  17.8 1.0 select_reduce_fusion
  18.8 0.1 multiply_reduce_fusion.2
  19.0 0.1 add_compare_fusion
  19.1 18.6 %all-to-all-done = bf16[32,16,1536]{2,1,0:T(8,128)(2,1)S(1)} async-done(((bf16[32,16,1536]{2,1,0:T(8,128)(2,1)}), bf16[32,16,1536]{2,1,0:T(8,128)(2,1)S(1)}, u32[]{:S(2)}, u32[]{:S(2)}) %all-to-all-start) | async-done | bytes 1572896 | tf_op jit(solution)/shard_map/all_to_all | solution.py:27
  37.7 0.6 gather_fusion
  38.3 0.0 copy-done
  38.3 0.3 convolution_convert_fusion
  38.6 0.1 reshape.237
  38.8 0.1 multiply_reduce_fusion.1
  38.9 0.1 copy.28
  38.9 0.8 gather_fusion.1
  39.8 3.8 %fusion.39 = (f32[192,2]{1,0:T(8,128)S(1)}, f32[192,2,128]{2,1,0:T(2,128)S(1)}) fusion(bf16[192,2,1,96,128]{4,3,2,1,0:T(8,128)(2,1)} %param.12, bf16[192,2,96]{2,1,0:T(2,128)(2,1)S(1)} %gather_fusion.1, pred[192]{0:T(512)(128)(4,1)S(1)} %compare_and_fusion.1, pred[192,128]{1,0:T(8,128)(4,1)S(1)} %add_compare_fusion), kind=kOutput, calls=%fused_computation.76 | convolution fusion | flops 9621120 | bytes 5015232 | tf_op jit(solution)/shard_map/pgjd,pgdt->pgjt/dot_general | solution.py:52
  43.6 0.1 copy.27
  43.7 0.1 select_reduce_fusion.1
  43.8 0.1 copy.29
  43.9 0.7 gather_fusion.2
  44.6 0.1 broadcast_select_fusion.2
  44.7 0.0 copy-start.1
  44.7 5.0 %fusion = f32[192,2,96]{2,1,0:T(2,128)S(1)} fusion(bf16[192,2,1,96,128]{4,3,2,1,0:T(8,128)(2,1)} %param.12, f32[192,2,128]{2,1,0:T(2,128)S(1)} %get-tuple-element.16, f32[192,2]{1,0:T(8,128)S(1)} %broadcast_select_fusion.2), kind=kOutput, calls=%fused_computation.3 | convolution fusion | flops 9535488 | bytes 5064192 | tf_op jit(solution)/shard_map/pgjt,pgdt->pgjd/dot_general | solution.py:69
  49.7 0.5 fusion.16
  50.3 0.0 copy-start.2
  50.3 0.3 convolution_add_fusion.1
  50.5 0.3 fusion.11
  50.8 0.1 reshape.240
  50.9 24.9 %all_gather.3 = bf16[512,192]{1,0:T(8,128)(2,1)S(1)} all-gather(bf16[16,192]{1,0:T(8,128)(2,1)S(1)} %reshape.240), channel_id=1, replica_groups=mesh['req'=32,'kv'=8] {'req'}, dimensions={0}, use_global_device_ids=true | all-gather | bytes 202752 | tf_op jit(solution)/shard_map/all_gather | solution.py:84
  75.8 0.0 copy-done.1
  75.8 1.5 %convolution_bitcast_fusion = f32[1536,16]{1,0:T(8,128)} fusion(bf16[1536,192]{0,1:T(8,128)(2,1)S(1)} %copy-done.1, bf16[512,192]{1,0:T(8,128)(2,1)S(1)} %all_gather.3, s32[512]{0:T(512)S(1)} %copy-done.4, s32[16]{0:T(128)S(1)} %iota_add_fusion), kind=kOutput, calls=%fused_computation.9 | convolution fusion | flops 12594176 | bytes 886848
  77.3 0.0 reduce-scatter.4.cloned.1.call-update
  77.3 0.0 copy-done.2
  77.3 39.3 %reduce-scatter.4.cloned.1.call-done = f32[192,16]{1,0:T(8,128)} async-done(((f32[1536,16]{1,0:T(8,128)}), f32[192,16]{1,0:T(8,128)}) %reduce-scatter.4.cloned.1.call-update) | async-done | bytes 12304
  116.7 0.9 copy.34
  117.6 0.7 add_convert_fusion
  (15 shorter events, 0.1 us)
Async XLA Ops:
  6.5 31.8 %copy-start = (bf16[1536,384]{1,0:T(8,128)(2,1)S(1)}, bf16[1536,384]{1,0:T(8,128)(2,1)}, u32[]{:S(2)}) copy-start(bf16[1536,384]{1,0:T(8,128)(2,1)} %param.10) | copy-start | bytes 3538948
  9.8 7.8 %copy-start.4 = (s32[512]{0:T(512)S(1)}, s32[512]{0:T(512)}, u32[]{:S(2)}) copy-start(s32[512]{0:T(512)} %param.15) | copy-start | bytes 6148
  9.8 7.9 %copy-start.5 = (s32[16]{0:T(128)S(1)}, s32[16]{0:T(128)}, u32[]{:S(2)}) copy-start(s32[16]{0:T(128)} %param.13) | copy-start | bytes 196
  9.8 8.0 %copy-start.3 = (s32[16,128]{1,0:T(8,128)S(1)}, s32[16,128]{1,0:T(8,128)}, u32[]{:S(2)}) copy-start(s32[16,128]{1,0:T(8,128)} %param.14) | copy-start | bytes 24580
  9.8 27.9 %all-to-all-start = ((bf16[32,16,1536]{2,1,0:T(8,128)(2,1)}), bf16[32,16,1536]{2,1,0:T(8,128)(2,1)S(1)}, u32[]{:S(2)}, u32[]{:S(2)}) async-start(bf16[32,16,1536]{2,1,0:T(8,128)(2,1)} %tile.2), calls=%async_computation | async-start | bytes 3145728 | tf_op jit(solution)/shard_map/all_to_all | solution.py:27
  17.6 99.1 %reduce-scatter.4.cloned.1.call-start = ((), (), s32[]{:S(2)}) async-start(), calls=%async_computation.2 | async-start | bytes 884736
  44.7 31.1 %copy-start.1 = (bf16[1536,192]{0,1:T(8,128)(2,1)S(1)}, bf16[1536,192]{0,1:T(8,128)(2,1)}, u32[]{:S(2)}) copy-start(bf16[1536,192]{0,1:T(8,128)(2,1)} %param.11) | copy-start | bytes 1769476
  50.3 27.0 %copy-start.2 = (bf16[16,1536]{1,0:T(8,128)(2,1)S(1)}, bf16[16,1536]{1,0:T(8,128)(2,1)}, u32[]{:S(2)}) copy-start(bf16[16,1536]{1,0:T(8,128)(2,1)} %param.8) | copy-start | bytes 147460
Sparse Core Ops, SparseCore 0:
  77.4 39.1 reduce-scatter.3
